TPU v7x, 256 devices: a whole 4x4x8 slice. The times are simulated.
256 devices in a mesh: role: 2 (over core), dp: 16 (over x, y), tensor: 8 (over z).
Axes of the slice: x: 4, y: 4, z: 8, core: 2. Of those that a mesh axis runs over, the one named last changes fastest.
Arguments:
- queries: bfloat16 [1024, 128, 576], P(('dp', 'tensor'), 'role'), may hold values from -13 to 13
- latent_cache: bfloat16 [512, 1024, 576], P(('dp', 'tensor')), may hold values from -4 to 4
- new_latent: bfloat16 [1024, 576], P(('dp', 'tensor')), may hold values from -9 to 9
- cache_lengths: int32 [512], P(('dp', 'tensor')), may hold values from 2 to 1024
- value_proj: bfloat16 [128, 512, 128], P(('role', 'tensor')), may hold values from -1 to 1
- out_proj: bfloat16 [16384, 7168], P(('role', 'tensor'), 'dp'), may hold values from -0.046875 to 0.046875
- residual: bfloat16 [1024, 7168], P(('role', 'tensor'), 'dp'), may hold values from -68 to 68
- norm_gain: bfloat16 [7168], replicated, may hold values from 0.5 to 1.5
- routes: int32 [1024, 8], P(('role', 'tensor')), may hold values from 0 to 15, all different within a row; in each aligned block of 64 rows (0 to 63, 64 to 127, ...) at most 40 rows name the same one
- gate_values: float32 [1024, 8], P(('role', 'tensor')), may hold values from 0.2 to 0.8
- tenant_ids: int32 [1024], P(('role', 'tensor')), may hold values from 0 to 2
- expert_gate_weight: bfloat16 [16, 7168, 2048], P('dp', None, ('role', 'tensor')), may hold values from -0.0625 to 0.0625
- expert_up_weight: bfloat16 [16, 7168, 2048], P('dp', None, ('role', 'tensor')), may hold values from -0.0625 to 0.0625
- expert_down_weight: bfloat16 [16, 2048, 7168], P('dp', ('role', 'tensor')), may hold values from -0.125 to 0.125
- left_delta_factor: bfloat16 [3, 16, 2048, 64], P(None, 'dp', ('role', 'tensor')), may hold values from -0.125 to 0.125
- factor_right: bfloat16 [3, 16, 64, 7168], P(None, 'dp'), may hold values from -0.75 to 0.75
Outputs:
- mixed: bfloat16 [1024, 7168], P(('role', 'tensor'), 'dp')
Inputs may be any that keep to these rules, and one draw needn't show every extreme that they name: `routes`: in each aligned block of 64 tokens no expert is named by more than 40 of them.
All inputs are finite; a program needn't handle non-finite values.
Results may differ from a plain program's by a relative error of at most 0.008.
Values may be sent and summed in bfloat16 or wider, within the bound.
No kernel may reach another device: no remote copies, remote signals or barrier semaphores. Data moves between devices by JAX's collectives and lax.ppermute only.
A program may use at most 128 MiB of HBM per device.

v0:
```python
import jax
import jax.numpy as jnp
from jax import lax
from jax.sharding import PartitionSpec as P

LAT = 512
EXPERTS = 16
TEN = 3
SCORE_SCALE = 0.07216878364870323
NORM_EPS = 1e-06
MASKED = -1e30


def rms_rows(input_rows, norm_gain):
    wide = input_rows.astype(jnp.float32)
    scale = lax.rsqrt(jnp.mean(wide * wide, axis=-1, keepdims=True) + NORM_EPS)
    return (wide * scale * norm_gain.astype(jnp.float32)).astype(jnp.bfloat16)


def local(
    queries,
    latent_cache,
    new_latent,
    cache_lengths,
    value_proj,
    out_proj,
    residual,
    norm_gain,
    routes,
    gate_values,
    tenant_ids,
    expert_gate_weight,
    expert_up_weight,
    expert_down_weight,
    left_delta_factor,
    factor_right,
):
    seq_count, context, width = latent_cache.shape
    local_heads = queries.shape[1]
    paired = queries.reshape(seq_count, 2, local_heads, width)
    scores = (
        jnp.einsum("sqhd,spd->sqhp", paired, latent_cache, preferred_element_type=jnp.float32)
        * SCORE_SCALE
    )
    present = jnp.arange(context, dtype=jnp.int32)[None, :] < cache_lengths[:, None]
    scores = jnp.where(present[:, None, None, :], scores, MASKED)
    fresh_keys = new_latent.reshape(seq_count, 2, width)
    fresh = (
        jnp.einsum("sqhd,skd->sqhk", paired, fresh_keys, preferred_element_type=jnp.float32)
        * SCORE_SCALE
    )
    causal = jnp.arange(2)[:, None] >= jnp.arange(2)[None, :]
    fresh = jnp.where(causal[None, :, None, :], fresh, MASKED)
    top = jnp.maximum(jnp.max(scores, axis=3), jnp.max(fresh, axis=3))[..., None]
    weights = jnp.exp(scores - top)
    fresh_weights = jnp.exp(fresh - top)
    total = jnp.sum(weights, axis=3) + jnp.sum(fresh_weights, axis=3)
    summed = jnp.einsum(
        "sqhp,spd->sqhd",
        weights.astype(jnp.bfloat16),
        latent_cache[:, :, :LAT],
        preferred_element_type=jnp.float32,
    )
    summed = summed + jnp.einsum(
        "sqhk,skd->sqhd",
        fresh_weights.astype(jnp.bfloat16),
        fresh_keys[:, :, :LAT],
        preferred_element_type=jnp.float32,
    )
    attended = (
        (summed / total[..., None]).astype(jnp.bfloat16).reshape(seq_count * 2, local_heads, LAT)
    )
    by_head = lax.all_to_all(attended, "tensor", split_axis=1, concat_axis=0, tiled=True)
    head_values = jnp.einsum(
        "thl,hlv->thv", by_head, value_proj, preferred_element_type=jnp.float32
    ).astype(jnp.bfloat16)
    head_values = head_values.reshape(
        head_values.shape[0], head_values.shape[1] * head_values.shape[2]
    )
    all_values = lax.all_gather(head_values, "dp", axis=0, tiled=True)
    group_rows = residual.shape[0]
    input_rows = all_values
    attention = lax.psum_scatter(
        jnp.dot(input_rows, out_proj, preferred_element_type=jnp.float32),
        ("role", "tensor"),
        scatter_dimension=0,
        tiled=True,
    )
    mixed_in = lax.optimization_barrier(
        (residual.astype(jnp.float32) + attention).astype(jnp.bfloat16)
    )
    capacity = 5 * group_rows // 8
    labels = jnp.arange(EXPERTS, dtype=jnp.int32)
    chosen = (routes[:, :, None] == labels[None, None, :]).astype(jnp.int32)
    routed = jnp.sum(chosen, axis=1)
    earlier = jnp.cumsum(routed, axis=0) - routed
    slot_ids = jnp.arange(capacity, dtype=jnp.int32)
    table = (routed.T[:, None, :] > 0) & (earlier.T[:, None, :] == slot_ids[None, :, None])
    local_experts = EXPERTS // lax.axis_size("dp")
    expert_start = lax.axis_index("dp") * local_experts
    mine = lax.dynamic_slice_in_dim(table, expert_start, local_experts, 0)
    full_rows = lax.all_gather(mixed_in, "dp", axis=1, tiled=True)
    picked = jnp.einsum(
        "ecg,gd->ecd", mine.astype(jnp.bfloat16), full_rows, preferred_element_type=jnp.float32
    ).astype(jnp.bfloat16)
    slot_rows = rms_rows(picked, norm_gain)
    slot_owner = jnp.sum(mine.astype(jnp.int32) * tenant_ids[None, None, :], axis=2)
    collected_rows, owners = (
        lax.all_gather(slot_rows, ("role", "tensor"), axis=1, tiled=True),
        lax.all_gather(slot_owner, ("role", "tensor"), axis=1, tiled=True),
    )
    gate_scores = jnp.einsum(
        "gpc,gcb->gpb", collected_rows, expert_gate_weight, preferred_element_type=jnp.float32
    )
    upper_bound = jnp.einsum(
        "gpc,gcb->gpb", collected_rows, expert_up_weight, preferred_element_type=jnp.float32
    )
    hidden = (jax.nn.silu(gate_scores) * upper_bound).astype(jnp.bfloat16)
    owner_mask = (owners[:, :, None] == jnp.arange(TEN, dtype=jnp.int32)[None, None, :]).astype(
        jnp.float32
    )
    widened_right_factor = factor_right.astype(jnp.float32)
    input_rows = hidden
    base_output = jnp.einsum(
        "xog,xgm->oxm", input_rows, expert_down_weight, preferred_element_type=jnp.float32
    )
    mixing_coefficient = (
        jnp.einsum(
            "ywv,oyvh->ywoh", input_rows, left_delta_factor, preferred_element_type=jnp.float32
        )
        * owner_mask[..., None]
    )
    outputs = lax.psum_scatter(
        base_output
        - jnp.einsum(
            "okei,eoiw->kow",
            mixing_coefficient,
            widened_right_factor,
            precision=lax.Precision.HIGHEST,
        ),
        ("role", "tensor"),
        scatter_dimension=0,
        tiled=True,
    ).astype(jnp.bfloat16)
    gate_of = jnp.sum(gate_values[:, :, None] * chosen.astype(jnp.float32), axis=1)
    weighting = table.astype(jnp.float32) * gate_of.T[:, None, :]
    own_weights = lax.dynamic_slice_in_dim(weighting, expert_start, local_experts, 0)
    token_terms = jnp.einsum(
        "lcg,cld->gd", own_weights, outputs.astype(jnp.float32), precision=lax.Precision.HIGHEST
    )
    expert_part = lax.psum_scatter(token_terms, "dp", scatter_dimension=1, tiled=True)
    return (mixed_in.astype(jnp.float32) + expert_part).astype(jnp.bfloat16)


def solution(mesh):
    placed = (
        P(("dp", "tensor"), "role", None),
        P(("dp", "tensor"), None, None),
        P(("dp", "tensor"), None),
        P(("dp", "tensor")),
        P(("role", "tensor"), None, None),
        P(("role", "tensor"), "dp"),
        P(("role", "tensor"), "dp"),
        P(),
        P(("role", "tensor"), None),
        P(("role", "tensor"), None),
        P(("role", "tensor")),
        P("dp", None, ("role", "tensor")),
        P("dp", None, ("role", "tensor")),
        P("dp", ("role", "tensor"), None),
        P(None, "dp", ("role", "tensor"), None),
        P(None, "dp", None, None),
    )
    return jax.shard_map(
        local, mesh=mesh, in_specs=placed, out_specs=P(("role", "tensor"), "dp"), check_vma=False
    )
```

profile of v0, /device:TPU:2, one launch (start us, length us, event | category | flops | bytes accessed | tf_op | source)
XLA Modules:
  0.0 579.4 jit_solution(11137241923393458110)
XLA Ops:
  6.5 0.9 iota_compare_fusion.2
  8.2 3.9 fusion.8
  13.2 2.5 fusion.4
  15.8 1.7 fusion.18
  17.8 25.8 %all_to_all.18 = bf16[8,64,512]{2,0,1:T(8,128)(2,1)S(1)} all-to-all(bf16[8,64,512]{2,0,1:T(8,128)(2,1)S(1)} %copy.41), channel_id=1, replica_groups=mesh['role'=2,'dp'=16,'tensor'=8] {'tensor'}, dimensions={1} | all-to-all | bytes 1048576 | tf_op jit(solution)/shard_map/all_to_all | solution.py:73
  44.6 46.0 %all-gather.6.cloned.1.call-done = bf16[1024,1024]{1,0:T(8,128)(2,1)} async-done(((bf16[64,1024]{1,0:T(8,128)(2,1)}), bf16[1024,1024]{1,0:T(8,128)(2,1)}) %all-gather.6.cloned.1.call-update) | async-done | bytes 2097168 | tf_op jit(solution)/shard_map/all_gather | solution.py:80
  90.6 4.4 fusion.60
  96.1 65.1 %reduce-scatter.6.cloned.1.call-done = f32[64,448]{1,0:T(8,128)} async-done(((f32[1024,448]{1,0:T(8,128)}), f32[64,448]{1,0:T(8,128)}) %reduce-scatter.6.cloned.1.call-update) | async-done | bytes 114704 | tf_op jit(solution)/shard_map/reduce_scatter | solution.py:83
  161.2 0.9 add_convert_fusion.1
  162.1 24.2 %all-gather.2 = bf16[16,448,64]{1,2,0:T(8,128)(2,1)S(1)} all-gather(bf16[1,448,64]{1,2,0:T(8,128)(2,1)S(1)} %bitcast.111), channel_id=1, replica_groups=mesh['role'=2,'dp'=16,'tensor'=8] {'dp'}, dimensions={0}, use_global_device_ids=true | all-gather | bytes 974848 | tf_op jit(solution)/shard_map/all_gather | solution.py:102
  186.3 1.6 copy.47
  187.8 2.9 reshape.187
  190.8 1.6 multiply_reduce_fusion
  192.4 1.0 multiply_convert_fusion
  195.1 13.6 %all-reduce = s32[640]{0:T(1024)S(1)} all-reduce(s32[640]{0:T(1024)S(1)} %dynamic-update-slice), channel_id=3, replica_groups=mesh['role'=2,'dp'=16,'tensor'=8] {'role','tensor'}, use_global_device_ids=true, to_apply=%add | all-reduce | flops 640 | bytes 5120
  208.7 43.6 %all-gather.8.cloned.1.call-done = bf16[640,7168]{1,0:T(8,128)(2,1)} async-done(((bf16[40,7168]{1,0:T(8,128)(2,1)}), bf16[640,7168]{1,0:T(8,128)(2,1)}) %all-gather.8.cloned.1.call-update) | async-done | bytes 9175056 | tf_op jit(solution)/shard_map/all_gather | solution.py:109
  252.3 6.8 %fusion.13 = f32[640,128]{1,0:T(8,128)S(1)} fusion(bf16[640,7168]{1,0:T(8,128)(2,1)} %all-gather.8.cloned.1.call-done, bf16[1,7168,128]{2,1,0:T(8,128)(2,1)} %param.27), kind=kOutput, calls=%fused_computation.18 | convolution fusion | flops 1174405120 | bytes 11337728 | tf_op jit(solution)/shard_map/gpc,gcb->gpb/dot_general | solution.py:112
  259.5 2.6 fusion.22
  262.1 8.8 %fusion.9 = f32[640,7168]{1,0:T(8,128)} fusion(bf16[640,128]{1,0:T(8,128)(2,1)S(1)} %fusion.22, bf16[1,128,7168]{2,1,0:T(8,128)(2,1)S(1)} %copy-done.1), kind=kOutput, calls=%fused_computation.14 | convolution fusion | flops 1174405120 | bytes 20348928 | tf_op jit(solution)/shard_map/xog,xgm->oxm/dot_general | solution.py:124
  271.2 14.8 %fusion = f32[640,1,7168]{2,0,1:T(8,128)} fusion(f32[640,7168]{1,0:T(8,128)} %fusion.9, bf16[3,1,64,7168]{3,2,1,0:T(8,128)(2,1)S(1)} %copy-done, f32[640,3,64]{0,2,1:T(8,128)S(1)} %bitcast.107, f32[640,3]{0,1:T(4,128)S(1)} %fusion.47), kind=kOutput, calls=%fused_computation.1 | convolution fusion | flops 10574356480 | bytes 39951872 | tf_op jit(solution)/shard_map/okei,eoiw->kow/dot_general | solution.py:135
  286.7 198.2 %reduce-scatter.8.cloned.1.call-done = f32[40,1,7168]{2,0,1:T(8,128)} async-done(((f32[640,1,7168]{2,0,1:T(8,128)}), f32[40,1,7168]{2,0,1:T(8,128)}) %reduce-scatter.8.cloned.1.call-update) | async-done | bytes 1146896 | tf_op jit(solution)/shard_map/reduce_scatter | solution.py:133
  485.0 5.1 convolution_bitcast_fusion
  490.0 81.2 %reduce-scatter.10.cloned.1.call-done = f32[448,64]{1,0:T(8,128)} async-done(((f32[7168,64]{1,0:T(8,128)}), f32[448,64]{1,0:T(8,128)}) %reduce-scatter.10.cloned.1.call-update) | async-done | bytes 114704
  571.2 1.0 copy.53
  (72 shorter events, 7.3 us)
Async XLA Ops:
  6.5 264.6 %copy-start = (bf16[3,1,64,7168]{3,2,1,0:T(8,128)(2,1)S(1)}, bf16[3,1,64,7168]{3,2,1,0:T(8,128)(2,1)}, u32[]{:S(2)}) copy-start(bf16[3,1,64,7168]{3,2,1,0:T(8,128)(2,1)} %param.31) | copy-start | bytes 8257540
  6.5 84.1 %all-gather.6.cloned.1.call-start = ((), (), s32[]{:S(2)}) async-start(), calls=%async_computation.4 | async-start | bytes 2228224 | tf_op jit(solution)/shard_map/all_gather | solution.py:80
  8.1 5.0 slice-start
  8.1 3.9 copy-start.3
  8.2 5.0 slice-start.1
  13.2 2.6 copy-start.6
  15.8 27.8 %copy-start.2 = (bf16[8,512,128]{2,1,0:T(8,128)(2,1)S(1)}, bf16[8,512,128]{2,1,0:T(8,128)(2,1)}, u32[]{:S(2)}) copy-start(bf16[8,512,128]{2,1,0:T(8,128)(2,1)} %param.20) | copy-start | bytes 3145732
  44.6 116.6 %reduce-scatter.6.cloned.1.call-start = ((), (), s32[]{:S(2)}) async-start(), calls=%async_computation.5 | async-start | bytes 2228224 | tf_op jit(solution)/shard_map/reduce_scatter | solution.py:83
  95.0 0.7 copy-start.7
  95.0 1.0 copy-start.8
  95.0 66.2 %copy-start.4 = (bf16[64,448]{1,0:T(8,128)(2,1)S(1)}, bf16[64,448]{1,0:T(8,128)(2,1)}, u32[]{:S(2)}) copy-start(bf16[64,448]{1,0:T(8,128)(2,1)} %param.22) | copy-start | bytes 172036
  95.0 157.3 %all-gather.8.cloned.1.call-start = ((), (), s32[]{:S(2)}) async-start(), calls=%async_computation.7 | async-start | bytes 9748480 | tf_op jit(solution)/shard_map/all_gather | solution.py:109
  190.8 2.7 copy-start.13
  190.8 4.0 copy-start.10
  193.4 291.5 %reduce-scatter.8.cloned.1.call-start = ((), (), s32[]{:S(2)}) async-start(), calls=%async_computation.6 | async-start | bytes 19496960 | tf_op jit(solution)/shard_map/reduce_scatter | solution.py:133
  252.3 6.8 %copy-start.11 = (bf16[640,7168]{1,0:T(8,128)(2,1)S(1)}, bf16[640,7168]{1,0:T(8,128)(2,1)}, u32[]{:S(2)}) copy-start(bf16[640,7168]{1,0:T(8,128)(2,1)} %all-gather.8.cloned.1.call-done) | copy-start | bytes 27525124
  252.3 7.2 %copy-start.12 = (bf16[1,7168,128]{2,1,0:T(8,128)(2,1)S(1)}, bf16[1,7168,128]{2,1,0:T(8,128)(2,1)}, u32[]{:S(2)}) copy-start(bf16[1,7168,128]{2,1,0:T(8,128)(2,1)} %param.28) | copy-start | bytes 5505028
  259.5 2.6 copy-start.1
  262.1 8.8 %copy-start.5 = (bf16[3,1,128,64]{2,3,1,0:T(8,128)(2,1)S(1)}, bf16[3,1,128,64]{2,3,1,0:T(8,128)(2,1)}, u32[]{:S(2)}) copy-start(bf16[3,1,128,64]{2,3,1,0:T(8,128)(2,1)} %param.30) | copy-start | bytes 147460
  286.0 0.7 copy-start.9
  286.0 285.2 %reduce-scatter.10.cloned.1.call-start = ((), (), s32[]{:S(2)}) async-start(), calls=%async_computation.8 | async-start | bytes 3899392
Sparse Core Ops, SparseCore 0:
  44.7 45.9 all-gather.5
  95.2 65.9 reduce-scatter.5
  193.5 58.7 all-gather.7
  286.1 198.7 reduce-scatter.7
  490.2 80.9 reduce-scatter.9
where the time goes:
time: 580 us; the launch traced here: 579 us
  waiting for transfers between devices  434 us (75%)
  blocking collectives  63.5 us (11%)
  matrix products  53.1 us (9%)
  between operations  14.1 us (2%)
  local copies, waits for them, and re-layouts  9.95 us (2%)
    reduce_scatter x1, waiting for transfers between devices, local(): lax.psum_scatter(base_output - jnp.einsum('okei,eoiw->kow', mixing_coeffi...  198 us
    unnamed x6, waiting for transfers between devices  81.2 us
    reduce_scatter x1, waiting for transfers between devices, local(): lax.psum_scatter(jnp.dot(input_rows, out_proj, preferred_element_type=jnp...  65.1 us
    all_gather x1, waiting for transfers between devices, local(): all_values = lax.all_gather(head_values, 'dp', axis=0, tiled=True)  46 us
    all_gather x1, waiting for transfers between devices, local(): lax.all_gather(slot_rows, ('role', 'tensor'), axis=1, tiled=True)  43.6 us
    all_to_all x1, blocking collectives, local(): lax.all_to_all(attended, 'tensor', split_axis=1, concat_axis=0, tiled=True)  25.8 us
    all_gather x1, blocking collectives, local(): full_rows = lax.all_gather(mixed_in, 'dp', axis=1, tiled=True)  24.2 us
    dot_general x1, matrix products, local(): jnp.einsum('okei,eoiw->kow', mixing_coefficient, widened_right_factor, pr...  14.8 us
  transfers between devices with their start and end apart: 5, of which 5 were waited for; matrix products, arithmetic and copies ran while one was open for 0% of the time, Pallas kernels for 0%

commit v1 on v0

--- a/solution.py
+++ b/solution.py
@@ -9,6 +9,24 @@
 SCORE_SCALE = 0.07216878364870323
 NORM_EPS = 1e-06
 MASKED = -1e30
+
+
+def ring_gather(array, axis, dim):
+    ways, here, step = (lax.axis_size(axis), lax.axis_index(axis), array.shape[dim])
+    shape = [n * ways if d == dim else n for d, n in enumerate(array.shape)]
+    full = lax.dynamic_update_slice_in_dim(
+        jnp.zeros(shape, array.dtype), array, here * step, axis=dim
+    )
+    going_up = going_down = array
+    for far in range(1, ways // 2 + 1):
+        going_up = lax.ppermute(going_up, axis, [(d, (d + 1) % ways) for d in range(ways)])
+        full = lax.dynamic_update_slice_in_dim(full, going_up, (here - far) % ways * step, axis=dim)
+        if 2 * far < ways:
+            going_down = lax.ppermute(going_down, axis, [(d, (d - 1) % ways) for d in range(ways)])
+            full = lax.dynamic_update_slice_in_dim(
+                full, going_down, (here + far) % ways * step, axis=dim
+            )
+    return full
 
 
 def rms_rows(input_rows, norm_gain):
@@ -77,7 +95,7 @@
     head_values = head_values.reshape(
         head_values.shape[0], head_values.shape[1] * head_values.shape[2]
     )
-    all_values = lax.all_gather(head_values, "dp", axis=0, tiled=True)
+    all_values = ring_gather(head_values, "dp", 0)
     group_rows = residual.shape[0]
     input_rows = all_values
     attention = lax.psum_scatter(

time: 580 us -> 594 us (1.024)
  starting transfers between devices: 0.17 us -> 37.9 us
  blocking collectives: 63.5 us -> 37.8 us
    all_gather x1 -> x0, waiting for transfers between devices: 46 us -> none  [local(): all_values = lax.all_gather(head_values, 'dp', axis=0, tiled=True)]
    ppermute x0 -> x15, starting transfers between devices: none -> 29.3 us  [the longest x7 27.6 us: ring_gather(): lax.ppermute(going_down, axis, [(d, (d - 1) % ways) for d in range(ways)])]
    ppermute x0 -> x15, waiting for transfers between devices: none -> 29 us  [the longest x8 28.9 us: ring_gather(): lax.ppermute(going_up, axis, [(d, (d + 1) % ways) for d in range(ways)])]
    all_to_all x1 -> x0, blocking collectives: 25.8 us -> none  [local(): lax.all_to_all(attended, 'tensor', split_axis=1, concat_axis=0, tiled=True)]
    all_to_all x0 -> x1, waiting for transfers between devices: none -> 17.2 us  [local(): lax.all_to_all(attended, 'tensor', split_axis=1, concat_axis=0, tiled=True)]
    all_to_all x0 -> x1, starting transfers between devices: none -> 8.46 us  [local(): lax.all_to_all(attended, 'tensor', split_axis=1, concat_axis=0, tiled=True)]
    unnamed x6 -> x5, waiting for transfers between devices: 81.2 us -> 81.1 us
  transfers between devices with their start and end apart: 5 -> 20, of which waited for: 5 -> 13; matrix products, arithmetic and copies ran while one was open for 0% -> 0% of each run, Pallas kernels for 0% -> 0%
where the time goes in v1:
time: 594 us; the launch traced here: 593 us
  waiting for transfers between devices  435 us (73%)
  matrix products  52.4 us (9%)
  starting transfers between devices  37.9 us (6%)
  blocking collectives  37.8 us (6%)
  between operations  14.5 us (2%)
  local copies, waits for them, and re-layouts  10.6 us (2%)
    reduce_scatter x1, waiting for transfers between devices, local(): lax.psum_scatter(base_output - jnp.einsum('okei,eoiw->kow', mixing_coeffi...  198 us
    unnamed x5, waiting for transfers between devices  81.1 us
    reduce_scatter x1, waiting for transfers between devices, local(): lax.psum_scatter(jnp.dot(input_rows, out_proj, preferred_element_type=jnp...  66.5 us
    all_gather x1, waiting for transfers between devices, local(): lax.all_gather(slot_rows, ('role', 'tensor'), axis=1, tiled=True)  43.4 us
    ppermute x8, waiting for transfers between devices, ring_gather(): lax.ppermute(going_up, axis, [(d, (d + 1) % ways) for d in range(ways)])  28.9 us
    ppermute x7, starting transfers between devices, ring_gather(): lax.ppermute(going_down, axis, [(d, (d - 1) % ways) for d in range(ways)])  27.6 us
    all_gather x1, blocking collectives, local(): full_rows = lax.all_gather(mixed_in, 'dp', axis=1, tiled=True)  24.2 us
    all_to_all x1, waiting for transfers between devices, local(): lax.all_to_all(attended, 'tensor', split_axis=1, concat_axis=0, tiled=True)  17.2 us
  transfers between devices with their start and end apart: 20, of which 13 were waited for; matrix products, arithmetic and copies ran while one was open for 0% of the time, Pallas kernels for 0%

profile of v1, /device:TPU:2, one launch (start us, length us, event | category | flops | bytes accessed | tf_op | source)
XLA Modules:
  0.0 593.1 jit_solution(11506151605904056844)
XLA Ops:
  8.2 3.9 fusion.8
  18.4 8.5 %all-to-all-start = ((bf16[8,64,512]{2,0,1:T(8,128)(2,1)}), bf16[8,64,512]{2,0,1:T(8,128)(2,1)S(1)}, u32[]{:S(2)}, u32[]{:S(2)}) async-start(bf16[8,64,512]{2,0,1:T(8,128)(2,1)} %copy.41), calls=%async_computation | async-start | bytes 1048576 | tf_op jit(solution)/shard_map/all_to_all | solution.py:91
  27.2 17.2 %all-to-all-done = bf16[8,64,512]{2,0,1:T(8,128)(2,1)S(1)} async-done(((bf16[8,64,512]{2,0,1:T(8,128)(2,1)}), bf16[8,64,512]{2,0,1:T(8,128)(2,1)S(1)}, u32[]{:S(2)}, u32[]{:S(2)}) %all-to-all-start) | async-done | bytes 524320 | tf_op jit(solution)/shard_map/all_to_all | solution.py:91
  50.5 3.1 collective-permute-done
  53.6 4.1 collective-permute-start.3
  60.7 4.1 collective-permute-start.5
  67.8 4.1 collective-permute-start.7
  74.8 4.1 collective-permute-start.9
  79.0 3.6 collective-permute-done.8
  82.6 4.4 collective-permute-start.11
  87.1 3.5 collective-permute-done.10
  90.6 4.1 collective-permute-start.13
  94.8 3.0 collective-permute-done.12
  97.8 7.0 %collective-permute-done.14 = bf16[64,1024]{1,0:T(8,128)(2,1)S(1)} collective-permute-done((bf16[64,1024]{1,0:T(8,128)(2,1)S(1)}, bf16[64,1024]{1,0:T(8,128)(2,1)S(1)}, u32[]{:S(2)}, u32[]{:S(2)}) %collective-permute-start.14) | collective-permute-done | bytes 131104 | tf_op jit(solution)/shard_map/ppermute | solution.py:22
  108.6 66.5 %reduce-scatter.6.cloned.1.call-done = f32[64,448]{1,0:T(8,128)} async-done(((f32[1024,448]{1,0:T(8,128)}), f32[64,448]{1,0:T(8,128)}) %reduce-scatter.6.cloned.1.call-update) | async-done | bytes 114704 | tf_op jit(solution)/shard_map/reduce_scatter | solution.py:101
  176.0 24.2 %all-gather.2 = bf16[16,448,64]{1,2,0:T(8,128)(2,1)S(1)} all-gather(bf16[1,448,64]{1,2,0:T(8,128)(2,1)S(1)} %bitcast.113), channel_id=1, replica_groups=mesh['role'=2,'dp'=16,'tensor'=8] {'dp'}, dimensions={0}, use_global_device_ids=true | all-gather | bytes 974848 | tf_op jit(solution)/shard_map/all_gather | solution.py:120
  209.0 13.6 %all-reduce = s32[640]{0:T(1024)S(1)} all-reduce(s32[640]{0:T(1024)S(1)} %dynamic-update-slice), channel_id=3, replica_groups=mesh['role'=2,'dp'=16,'tensor'=8] {'role','tensor'}, use_global_device_ids=true, to_apply=%add | all-reduce | flops 640 | bytes 5120
  222.6 43.4 %all-gather.5.cloned.1.call-done = bf16[640,7168]{1,0:T(8,128)(2,1)} async-done(((bf16[40,7168]{1,0:T(8,128)(2,1)}), bf16[640,7168]{1,0:T(8,128)(2,1)}) %all-gather.5.cloned.1.call-update) | async-done | bytes 9175056 | tf_op jit(solution)/shard_map/all_gather | solution.py:127
  266.0 6.8 %fusion.13 = f32[640,128]{1,0:T(8,128)S(1)} fusion(bf16[640,7168]{1,0:T(8,128)(2,1)} %all-gather.5.cloned.1.call-done, bf16[1,7168,128]{2,1,0:T(8,128)(2,1)} %param.27), kind=kOutput, calls=%fused_computation.18 | convolution fusion | flops 1174405120 | bytes 11337728 | tf_op jit(solution)/shard_map/gpc,gcb->gpb/dot_general | solution.py:130
  275.8 8.8 %fusion.9 = f32[640,7168]{1,0:T(8,128)} fusion(bf16[640,128]{1,0:T(8,128)(2,1)S(1)} %fusion.22, bf16[1,128,7168]{2,1,0:T(8,128)(2,1)S(1)} %copy-done.1), kind=kOutput, calls=%fused_computation.14 | convolution fusion | flops 1174405120 | bytes 20348928 | tf_op jit(solution)/shard_map/xog,xgm->oxm/dot_general | solution.py:142
  284.9 14.8 %fusion = f32[640,1,7168]{2,0,1:T(8,128)} fusion(f32[640,7168]{1,0:T(8,128)} %fusion.9, bf16[3,1,64,7168]{3,2,1,0:T(8,128)(2,1)S(1)} %copy-done, f32[640,3,64]{0,2,1:T(8,128)S(1)} %bitcast.109, f32[640,3]{0,1:T(4,128)S(1)} %fusion.47), kind=kOutput, calls=%fused_computation.1 | convolution fusion | flops 10574356480 | bytes 39951872 | tf_op jit(solution)/shard_map/okei,eoiw->kow/dot_general | solution.py:153
  300.4 198.2 %reduce-scatter.8.cloned.1.call-done = f32[40,1,7168]{2,0,1:T(8,128)} async-done(((f32[640,1,7168]{2,0,1:T(8,128)}), f32[40,1,7168]{2,0,1:T(8,128)}) %reduce-scatter.8.cloned.1.call-update) | async-done | bytes 1146896 | tf_op jit(solution)/shard_map/reduce_scatter | solution.py:151
  498.7 5.1 convolution_bitcast_fusion
  503.8 81.1 %reduce-scatter.10.cloned.1.call-done = f32[448,64]{1,0:T(8,128)} async-done(((f32[7168,64]{1,0:T(8,128)}), f32[448,64]{1,0:T(8,128)}) %reduce-scatter.10.cloned.1.call-update) | async-done | bytes 114704
  (117 shorter events, 41.2 us)
Async XLA Ops:
  6.5 278.4 %copy-start = (bf16[3,1,64,7168]{3,2,1,0:T(8,128)(2,1)S(1)}, bf16[3,1,64,7168]{3,2,1,0:T(8,128)(2,1)}, u32[]{:S(2)}) copy-start(bf16[3,1,64,7168]{3,2,1,0:T(8,128)(2,1)} %param.31) | copy-start | bytes 8257540
  18.4 26.0 %all-to-all-start = ((bf16[8,64,512]{2,0,1:T(8,128)(2,1)}), bf16[8,64,512]{2,0,1:T(8,128)(2,1)S(1)}, u32[]{:S(2)}, u32[]{:S(2)}) async-start(bf16[8,64,512]{2,0,1:T(8,128)(2,1)} %copy.41), calls=%async_computation | async-start | bytes 1048576 | tf_op jit(solution)/shard_map/all_to_all | solution.py:91
  26.9 148.2 %reduce-scatter.6.cloned.1.call-start = ((), (), s32[]{:S(2)}) async-start(), calls=%async_computation.4 | async-start | bytes 2228224 | tf_op jit(solution)/shard_map/reduce_scatter | solution.py:101
  46.0 7.6 %collective-permute-start = (bf16[64,1024]{1,0:T(8,128)(2,1)S(1)}, bf16[64,1024]{1,0:T(8,128)(2,1)S(1)}, u32[]{:S(2)}, u32[]{:S(2)}) collective-permute-start(bf16[64,1024]{1,0:T(8,128)(2,1)S(1)} %bitcast.116), channel_id=1, source_target_pairs={{0,8},{8,16},{16,24},{24,32},{32,40},{40,48},{48,56},{56,64},{64,7... | collective-permute-start | bytes 393224 | tf_op jit(solution)/shard_map/ppermute | solution.py:22
  47.6 6.0 %collective-permute-start.1 = (bf16[64,1024]{1,0:T(8,128)(2,1)S(1)}, bf16[64,1024]{1,0:T(8,128)(2,1)S(1)}, u32[]{:S(2)}, u32[]{:S(2)}) collective-permute-start(bf16[64,1024]{1,0:T(8,128)(2,1)S(1)} %bitcast.117), channel_id=1, source_target_pairs={{0,120},{8,0},{16,8},{24,16},{32,24},{40,32},{48,40},{56,48},{64,5... | collective-permute-start | bytes 393224 | tf_op jit(solution)/shard_map/ppermute | solution.py:25
  50.5 54.4 %copy-start.12 = (bf16[1024,448]{0,1:T(8,128)(2,1)S(1)}, bf16[1024,448]{0,1:T(8,128)(2,1)}, u32[]{:S(2)}) copy-start(bf16[1024,448]{0,1:T(8,128)(2,1)} %param.21) | copy-start | bytes 2752516
  53.6 7.1 %collective-permute-start.2 = (bf16[64,1024]{1,0:T(8,128)(2,1)S(1)}, bf16[64,1024]{1,0:T(8,128)(2,1)S(1)}, u32[]{:S(2)}, u32[]{:S(2)}) collective-permute-start(bf16[64,1024]{1,0:T(8,128)(2,1)S(1)} %collective-permute-done), channel_id=1, source_target_pairs={{0,8},{8,16},{16,24},{24,32},{32,40},{40,48},{48,56},{56,64},{64,7... | collective-permute-start | bytes 393224 | tf_op jit(solution)/shard_map/ppermute | solution.py:22
  53.6 7.1 %collective-permute-start.3 = (bf16[64,1024]{1,0:T(8,128)(2,1)S(1)}, bf16[64,1024]{1,0:T(8,128)(2,1)S(1)}, u32[]{:S(2)}, u32[]{:S(2)}) collective-permute-start(bf16[64,1024]{1,0:T(8,128)(2,1)S(1)} %collective-permute-done.1), channel_id=1, source_target_pairs={{0,120},{8,0},{16,8},{24,16},{32,24},{40,32},{48,40},{56,48},{64,5... | collective-permute-start | bytes 393224 | tf_op jit(solution)/shard_map/ppermute | solution.py:25
  60.7 7.1 %collective-permute-start.4 = (bf16[64,1024]{1,0:T(8,128)(2,1)S(1)}, bf16[64,1024]{1,0:T(8,128)(2,1)S(1)}, u32[]{:S(2)}, u32[]{:S(2)}) collective-permute-start(bf16[64,1024]{1,0:T(8,128)(2,1)S(1)} %collective-permute-done.2), channel_id=1, source_target_pairs={{0,8},{8,16},{16,24},{24,32},{32,40},{40,48},{48,56},{56,64},{64,7... | collective-permute-start | bytes 393224 | tf_op jit(solution)/shard_map/ppermute | solution.py:22
  60.7 7.1 %collective-permute-start.5 = (bf16[64,1024]{1,0:T(8,128)(2,1)S(1)}, bf16[64,1024]{1,0:T(8,128)(2,1)S(1)}, u32[]{:S(2)}, u32[]{:S(2)}) collective-permute-start(bf16[64,1024]{1,0:T(8,128)(2,1)S(1)} %collective-permute-done.3), channel_id=1, source_target_pairs={{0,120},{8,0},{16,8},{24,16},{32,24},{40,32},{48,40},{56,48},{64,5... | collective-permute-start | bytes 393224 | tf_op jit(solution)/shard_map/ppermute | solution.py:25
  67.7 7.1 %collective-permute-start.6 = (bf16[64,1024]{1,0:T(8,128)(2,1)S(1)}, bf16[64,1024]{1,0:T(8,128)(2,1)S(1)}, u32[]{:S(2)}, u32[]{:S(2)}) collective-permute-start(bf16[64,1024]{1,0:T(8,128)(2,1)S(1)} %collective-permute-done.4), channel_id=1, source_target_pairs={{0,8},{8,16},{16,24},{24,32},{32,40},{40,48},{48,56},{56,64},{64,7... | collective-permute-start | bytes 393224 | tf_op jit(solution)/shard_map/ppermute | solution.py:22
  67.8 7.1 %collective-permute-start.7 = (bf16[64,1024]{1,0:T(8,128)(2,1)S(1)}, bf16[64,1024]{1,0:T(8,128)(2,1)S(1)}, u32[]{:S(2)}, u32[]{:S(2)}) collective-permute-start(bf16[64,1024]{1,0:T(8,128)(2,1)S(1)} %collective-permute-done.5), channel_id=1, source_target_pairs={{0,120},{8,0},{16,8},{24,16},{32,24},{40,32},{48,40},{56,48},{64,5... | collective-permute-start | bytes 393224 | tf_op jit(solution)/shard_map/ppermute | solution.py:25
  74.8 7.8 %collective-permute-start.8 = (bf16[64,1024]{1,0:T(8,128)(2,1)S(1)}, bf16[64,1024]{1,0:T(8,128)(2,1)S(1)}, u32[]{:S(2)}, u32[]{:S(2)}) collective-permute-start(bf16[64,1024]{1,0:T(8,128)(2,1)S(1)} %collective-permute-done.6), channel_id=1, source_target_pairs={{0,8},{8,16},{16,24},{24,32},{32,40},{40,48},{48,56},{56,64},{64,7... | collective-permute-start | bytes 393224 | tf_op jit(solution)/shard_map/ppermute | solution.py:22
  74.8 7.8 %collective-permute-start.9 = (bf16[64,1024]{1,0:T(8,128)(2,1)S(1)}, bf16[64,1024]{1,0:T(8,128)(2,1)S(1)}, u32[]{:S(2)}, u32[]{:S(2)}) collective-permute-start(bf16[64,1024]{1,0:T(8,128)(2,1)S(1)} %collective-permute-done.7), channel_id=1, source_target_pairs={{0,120},{8,0},{16,8},{24,16},{32,24},{40,32},{48,40},{56,48},{64,5... | collective-permute-start | bytes 393224 | tf_op jit(solution)/shard_map/ppermute | solution.py:25
  82.6 8.0 %collective-permute-start.10 = (bf16[64,1024]{1,0:T(8,128)(2,1)S(1)}, bf16[64,1024]{1,0:T(8,128)(2,1)S(1)}, u32[]{:S(2)}, u32[]{:S(2)}) collective-permute-start(bf16[64,1024]{1,0:T(8,128)(2,1)S(1)} %collective-permute-done.8), channel_id=1, source_target_pairs={{0,8},{8,16},{16,24},{24,32},{32,40},{40,48},{48,56},{56,64},{64,7... | collective-permute-start | bytes 393224 | tf_op jit(solution)/shard_map/ppermute | solution.py:22
  82.6 8.0 %collective-permute-start.11 = (bf16[64,1024]{1,0:T(8,128)(2,1)S(1)}, bf16[64,1024]{1,0:T(8,128)(2,1)S(1)}, u32[]{:S(2)}, u32[]{:S(2)}) collective-permute-start(bf16[64,1024]{1,0:T(8,128)(2,1)S(1)} %collective-permute-done.9), channel_id=1, source_target_pairs={{0,120},{8,0},{16,8},{24,16},{32,24},{40,32},{48,40},{56,48},{64,5... | collective-permute-start | bytes 393224 | tf_op jit(solution)/shard_map/ppermute | solution.py:25
  90.6 7.1 %collective-permute-start.12 = (bf16[64,1024]{1,0:T(8,128)(2,1)S(1)}, bf16[64,1024]{1,0:T(8,128)(2,1)S(1)}, u32[]{:S(2)}, u32[]{:S(2)}) collective-permute-start(bf16[64,1024]{1,0:T(8,128)(2,1)S(1)} %collective-permute-done.10), channel_id=1, source_target_pairs={{0,8},{8,16},{16,24},{24,32},{32,40},{40,48},{48,56},{56,64},{64,7... | collective-permute-start | bytes 393224 | tf_op jit(solution)/shard_map/ppermute | solution.py:22
  90.6 7.2 %collective-permute-start.13 = (bf16[64,1024]{1,0:T(8,128)(2,1)S(1)}, bf16[64,1024]{1,0:T(8,128)(2,1)S(1)}, u32[]{:S(2)}, u32[]{:S(2)}) collective-permute-start(bf16[64,1024]{1,0:T(8,128)(2,1)S(1)} %collective-permute-done.11), channel_id=1, source_target_pairs={{0,120},{8,0},{16,8},{24,16},{32,24},{40,32},{48,40},{56,48},{64,5... | collective-permute-start | bytes 393224 | tf_op jit(solution)/shard_map/ppermute | solution.py:25
  97.8 7.1 %collective-permute-start.14 = (bf16[64,1024]{1,0:T(8,128)(2,1)S(1)}, bf16[64,1024]{1,0:T(8,128)(2,1)S(1)}, u32[]{:S(2)}, u32[]{:S(2)}) collective-permute-start(bf16[64,1024]{1,0:T(8,128)(2,1)S(1)} %collective-permute-done.12), channel_id=1, source_target_pairs={{0,8},{8,16},{16,24},{24,32},{32,40},{40,48},{48,56},{56,64},{64,7... | collective-permute-start | bytes 393224 | tf_op jit(solution)/shard_map/ppermute | solution.py:22
  107.5 67.6 %copy-start.3 = (bf16[64,448]{1,0:T(8,128)(2,1)S(1)}, bf16[64,448]{1,0:T(8,128)(2,1)}, u32[]{:S(2)}) copy-start(bf16[64,448]{1,0:T(8,128)(2,1)} %param.22) | copy-start | bytes 172036
  107.5 158.5 %all-gather.5.cloned.1.call-start = ((), (), s32[]{:S(2)}) async-start(), calls=%async_computation.6 | async-start | bytes 9748480 | tf_op jit(solution)/shard_map/all_gather | solution.py:127
  207.3 291.3 %reduce-scatter.8.cloned.1.call-start = ((), (), s32[]{:S(2)}) async-start(), calls=%async_computation.5 | async-start | bytes 19496960 | tf_op jit(solution)/shard_map/reduce_scatter | solution.py:151
  275.8 8.8 %copy-start.4 = (bf16[3,1,128,64]{2,3,1,0:T(8,128)(2,1)S(1)}, bf16[3,1,128,64]{2,3,1,0:T(8,128)(2,1)}, u32[]{:S(2)}) copy-start(bf16[3,1,128,64]{2,3,1,0:T(8,128)(2,1)} %param.30) | copy-start | bytes 147460
  299.7 285.1 %reduce-scatter.10.cloned.1.call-start = ((), (), s32[]{:S(2)}) async-start(), calls=%async_computation.7 | async-start | bytes 3899392
  (12 other events, 42.1 us)
Sparse Core Ops, SparseCore 0:
  107.7 67.4 reduce-scatter.5
  207.4 58.5 all-gather.4
  299.8 198.7 reduce-scatter.7
  503.9 80.9 reduce-scatter.9
